TPU v7x, 32 devices: a whole 2x2x4 slice. The times are simulated.
32 devices in a mesh: grp: 2 (over y), dp: 4 (over x, core), sp: 4 (over z).
Axes of the slice: x: 2, y: 2, z: 4, core: 2. Of those that a mesh axis runs over, the one named last changes fastest.
Arguments:
- rollout_rows: bfloat16 [4096, 5120], P(('grp', 'dp', 'sp')), parts along dimension 0, may hold values from -28 to 28
- routing: int32 [4096], P('grp'), parts along dimension 0, may hold values from 0 to 3, as said below
- segment_labels: int32 [8, 512], P(('grp', 'dp'), 'sp'), parts along dimension 0, may hold values from 0 to 3, never falling along the last dimension, each value on 1 to 256 neighbouring positions
- upstream: bfloat16 [8, 512, 4096], P(('grp', 'dp'), 'sp'), parts along dimension 0, may hold values from -24 to 24
- passes: int32 [32], P('grp'), parts along dimension 0, may hold values from 0 to 10
- group_ids: int32 [32], P('grp'), parts along dimension 0, may hold values from 0 to 1, as said below
Outputs:
- query_gradient: bfloat16 [8, 512, 4096], P(('grp', 'dp'), 'sp'), parts along dimension 0
- kv_grads: bfloat16 [8, 512, 1024], P(('grp', 'dp'), 'sp'), parts along dimension 0
There are 2 independent parts, one for each index of `grp`. A program takes and returns all parts, laid end to end along the dimension named above; each array names one. Nothing has to cross between parts.
Inputs may be any that keep to these rules, and one draw needn't show every extreme that they name: `routing`: among the rows of one column j (rows i with (i // 128) % (4) == j) every owner receives exactly 128 rows; the rows of one device go to each owner in numbers 0, 32 or 64, and every device sends exactly 64 rows to one owner. `group_ids`: every group holds exactly 8 completions.
All inputs are finite; a program needn't handle non-finite values.
Results may differ from a plain program's by a relative error of at most 0.012.
Values may be sent and summed in bfloat16 or wider, within the bound.
No kernel may reach another device: no remote copies, remote signals or barrier semaphores. Data moves between devices by JAX's collectives and lax.ppermute only.
A program may use at most 128 MiB of HBM per device.

v0:
```python
import math
import jax
import jax.numpy as jnp
import numpy as np
from jax import lax
from jax.sharding import PartitionSpec as P

QUERY_HEADS = 32
KEY_VALUE_HEADS = 4
HEAD_SIZE = 128
SEGS = 4
GROUP = 8
TESTS = 10


def slot_layout(row_list, sequence_split_size):
    token_rows = row_list.shape[0]
    per_dev = QUERY_HEADS // sequence_split_size
    query_group = QUERY_HEADS // KEY_VALUE_HEADS
    query_rows = row_list[:, : QUERY_HEADS * HEAD_SIZE].reshape(
        token_rows, sequence_split_size, per_dev * HEAD_SIZE
    )
    key_value_couples = row_list[:, QUERY_HEADS * HEAD_SIZE :].reshape(
        token_rows, 2, KEY_VALUE_HEADS, HEAD_SIZE
    )
    head_table = np.arange(sequence_split_size) * per_dev // query_group
    picked = jnp.transpose(key_value_couples[:, :, head_table, :], (0, 2, 1, 3)).reshape(
        token_rows, sequence_split_size, 2 * HEAD_SIZE
    )
    return jnp.concatenate([query_rows, picked], axis=2)


def group_advantage(passes, group_ids):
    reward = passes.astype(jnp.float32) / TESTS
    labels = jnp.arange(group_ids.shape[0] // GROUP, dtype=jnp.int32)
    member = (group_ids[:, None] == labels[None, :]).astype(jnp.float32)
    group_mean = jnp.sum(member * reward[:, None], axis=0) / jnp.sum(member, axis=0)
    return reward - jnp.sum(member * group_mean[None, :], axis=1)


def body(rollout_rows, routing, segment_labels, upstream, passes, group_ids):
    dp_size = lax.axis_size("dp")
    sequence_split_size = lax.axis_size("sp")
    dp_index = lax.axis_index("dp")
    sp_index = lax.axis_index("sp")
    token_rows = rollout_rows.shape[0]
    row_width = rollout_rows.shape[1]
    capacity = 2 * token_rows // dp_size
    per_dev = QUERY_HEADS // sequence_split_size
    seq_len = sequence_split_size * token_rows
    layout_plan = routing.reshape(dp_size, sequence_split_size, token_rows)
    column_plan = lax.dynamic_index_in_dim(layout_plan, sp_index, axis=1, keepdims=False)
    own_plan = lax.dynamic_index_in_dim(column_plan, dp_index, axis=0, keepdims=False)
    targets = jnp.arange(dp_size, dtype=jnp.int32)
    hit_table = (own_plan[:, None] == targets[None, :]).astype(jnp.int32)
    rank_rows = jnp.sum((jnp.cumsum(hit_table, axis=0) - 1) * hit_table, axis=1)
    slot_ids = own_plan * capacity + rank_rows
    positions = jnp.arange(token_rows, dtype=jnp.int32)
    outgoing = (
        jnp.zeros((dp_size * capacity, row_width), rollout_rows.dtype)
        .at[slot_ids]
        .set(rollout_rows)
    )
    arrived = lax.all_to_all(
        outgoing.reshape(dp_size, capacity, row_width),
        "dp",
        split_axis=0,
        concat_axis=0,
        tiled=True,
    )
    load_table = jnp.sum((column_plan == dp_index).astype(jnp.int32), axis=1)
    end_marks = jnp.cumsum(load_table)
    start_marks = end_marks - load_table
    source = jnp.sum((positions[:, None] >= end_marks[None, :]).astype(jnp.int32), axis=1)
    chosen_start = jnp.sum(
        jnp.where(source[:, None] == targets[None, :], start_marks[None, :], 0), axis=1
    )
    packed_tensor = arrived.reshape(dp_size * capacity, row_width)[
        source * capacity + positions - chosen_start
    ]
    regrouped = lax.all_to_all(
        slot_layout(packed_tensor, sequence_split_size),
        "sp",
        split_axis=1,
        concat_axis=0,
        tiled=True,
    )
    local_rows = regrouped.reshape(seq_len, regrouped.shape[2])
    full_seg = lax.all_gather(segment_labels, "sp", axis=1, tiled=True)[0]
    advantage = group_advantage(passes, group_ids)
    bin_adv = lax.dynamic_slice_in_dim(advantage, dp_index * SEGS, SEGS)
    own_seg = segment_labels[0]
    tok_adv = jnp.sum(
        jnp.where(
            own_seg[:, None] == jnp.arange(SEGS, dtype=jnp.int32)[None, :], bin_adv[None, :], 0.0
        ),
        axis=1,
    )
    weighted_result = (upstream[0].astype(jnp.float32) * tok_adv[:, None]).astype(jnp.bfloat16)
    grads_in = lax.all_to_all(
        weighted_result.reshape(token_rows, sequence_split_size, per_dev * HEAD_SIZE),
        "sp",
        split_axis=1,
        concat_axis=0,
        tiled=True,
    )
    grads_in = grads_in.reshape(seq_len, per_dev, HEAD_SIZE)
    query_rows = local_rows[:, : per_dev * HEAD_SIZE].reshape(seq_len, per_dev, HEAD_SIZE)
    key_matrix = local_rows[:, per_dev * HEAD_SIZE : (per_dev + 1) * HEAD_SIZE]
    value_matrix = local_rows[:, (per_dev + 1) * HEAD_SIZE :]
    block_rows = 512
    inv_root = 1.0 / math.sqrt(HEAD_SIZE)
    key_pos = jnp.arange(seq_len, dtype=jnp.int32)
    key_total = jnp.zeros((seq_len, HEAD_SIZE), jnp.float32)
    value_total = jnp.zeros((seq_len, HEAD_SIZE), jnp.float32)
    query_parts = []
    for block_start in range(0, seq_len, block_rows):
        block_end = block_start + block_rows
        query_block = query_rows[block_start:block_end]
        grad_block = grads_in[block_start:block_end]
        key_part = key_matrix[:block_end]
        value_part = value_matrix[:block_end]
        scores = (
            jnp.einsum("bhd,kd->hbk", query_block, key_part, preferred_element_type=jnp.float32)
            * inv_root
        )
        allowed = (full_seg[block_start:block_end, None] == full_seg[None, :block_end]) & (
            key_pos[None, :block_end] <= key_pos[block_start:block_end, None]
        )
        scores = jnp.where(allowed[None], scores, -1e30)
        row_top = jnp.max(scores, axis=2, keepdims=True)
        scaled_exp = jnp.exp(scores - row_top)
        weights = scaled_exp / jnp.sum(scaled_exp, axis=2, keepdims=True)
        weight_grads = jnp.einsum(
            "bhd,kd->hbk", grad_block, value_part, preferred_element_type=jnp.float32
        )
        row_dot = jnp.sum(weights * weight_grads, axis=2, keepdims=True)
        score_grads = (weights * (weight_grads - row_dot) * inv_root).astype(jnp.bfloat16)
        query_parts.append(
            jnp.einsum(
                "hbk,kd->bhd", score_grads, key_part, preferred_element_type=jnp.float32
            ).astype(jnp.bfloat16)
        )
        key_total = key_total.at[:block_end].add(
            jnp.einsum("hbk,bhd->kd", score_grads, query_block, preferred_element_type=jnp.float32)
        )
        value_total = value_total.at[:block_end].add(
            jnp.einsum(
                "hbk,bhd->kd",
                weights.astype(jnp.bfloat16),
                grad_block,
                preferred_element_type=jnp.float32,
            )
        )
    query_back = jnp.concatenate(query_parts, axis=0).reshape(
        sequence_split_size, token_rows, per_dev * HEAD_SIZE
    )
    query_gradient = lax.all_to_all(query_back, "sp", split_axis=0, concat_axis=2, tiled=True)
    partial_value = jnp.concatenate([key_total, value_total], axis=1).reshape(
        sequence_split_size, token_rows, 2 * HEAD_SIZE
    )
    key_value_pieces = lax.all_to_all(
        partial_value.astype(jnp.bfloat16), "sp", split_axis=0, concat_axis=0, tiled=True
    ).astype(partial_value.dtype)
    summed_total = jnp.sum(
        key_value_pieces.reshape(
            KEY_VALUE_HEADS, sequence_split_size // KEY_VALUE_HEADS, token_rows, 2, HEAD_SIZE
        ),
        axis=1,
    )
    kv_grads = (
        jnp.transpose(summed_total, (1, 2, 0, 3))
        .reshape(1, token_rows, 2 * KEY_VALUE_HEADS * HEAD_SIZE)
        .astype(jnp.bfloat16)
    )
    return (query_gradient, kv_grads)


def solution(mesh):
    return jax.shard_map(
        body,
        mesh=mesh,
        in_specs=(
            P(("grp", "dp", "sp"), None),
            P("grp"),
            P(("grp", "dp"), "sp"),
            P(("grp", "dp"), "sp", None),
            P("grp"),
            P("grp"),
        ),
        out_specs=(P(("grp", "dp"), "sp", None), P(("grp", "dp"), "sp", None)),
        check_vma=False,
    )
```

profile of v0, /device:TPU:0, one launch (start us, length us, event | category | flops | bytes accessed | tf_op | source)
XLA Modules:
  0.0 174.7 jit_solution(5603575321468290316)
XLA Ops:
  2.5 5.0 %scatter_custom_fusion = bf16[256,5120]{1,0:T(8,128)(2,1)} fusion(s32[128]{0:T(128)S(1)} %fusion.32, bf16[128,5120]{1,0:T(8,128)(2,1)} %param.16, bf16[]{:T(256)} %constant.129.clone.1), kind=kCustom, calls=%fused_computation.24 | custom fusion | bytes 2621952 | tf_op jit(solution)/shard_map/scatter | solution.py:62
  7.5 4.2 %all-to-all-start = ((bf16[4,64,5120]{2,1,0:T(8,128)(2,1)}), bf16[4,64,5120]{2,1,0:T(8,128)(2,1)S(1)}, u32[]{:S(2)}, u32[]{:S(2)}) async-start(bf16[4,64,5120]{2,1,0:T(8,128)(2,1)} %bitcast.131), calls=%async_computation | async-start | bytes 5242880 | tf_op jit(solution)/shard_map/all_to_all | solution.py:64
  11.8 3.7 %reshape.279 = f32[128,4,1024]{2,1,0:T(4,128)} reshape(bf16[1,128,4096]{2,1,0:T(8,128)(2,1)} %param.19) | data formatting | bytes 3145728 | tf_op jit(solution)/shard_map/convert_element_type | solution.py:99
  15.9 3.7 %fusion.11 = bf16[128,4,1024]{2,0,1:T(8,128)(2,1)} fusion(f32[128,4,1024]{2,1,0:T(4,128)} %reshape.279, f32[128]{0:T(128)S(1)} %select_reduce_fusion.2), kind=kLoop, calls=%fused_computation.20 | loop fusion | flops 1048576 | bytes 3146240 | tf_op jit(solution)/shard_map/convert_element_type | solution.py:99
  19.6 23.5 %all-to-all-done = bf16[4,64,5120]{2,1,0:T(8,128)(2,1)S(1)} async-done(((bf16[4,64,5120]{2,1,0:T(8,128)(2,1)}), bf16[4,64,5120]{2,1,0:T(8,128)(2,1)S(1)}, u32[]{:S(2)}, u32[]{:S(2)}) %all-to-all-start) | async-done | bytes 2621472 | tf_op jit(solution)/shard_map/all_to_all | solution.py:64
  43.1 5.7 %all-to-all-start.2 = ((bf16[128,4,1024]{2,0,1:T(8,128)(2,1)}), bf16[128,4,1024]{2,0,1:T(8,128)(2,1)}, u32[]{:S(2)}, u32[]{:S(2)}) async-start(bf16[128,4,1024]{2,0,1:T(8,128)(2,1)} %fusion.11), calls=%async_computation.2 | async-start | bytes 2097152 | tf_op jit(solution)/shard_map/all_to_all | solution.py:100
  50.1 2.4 %gather_fusion = bf16[128,5120]{1,0:T(8,128)(2,1)} fusion(bf16[256,5120]{1,0:T(8,128)(2,1)S(1)} %bitcast.129, s32[1024]{0:T(1024)S(1)} %pad_clamp_fusion.1), kind=kCustom, calls=%fused_computation | custom fusion | bytes 2621952 | tf_op jit(solution)/shard_map/gather | solution.py:78
  53.5 1.3 slice.52
  57.2 17.1 %all-to-all-done.2 = bf16[128,4,1024]{2,0,1:T(8,128)(2,1)} async-done(((bf16[128,4,1024]{2,0,1:T(8,128)(2,1)}), bf16[128,4,1024]{2,0,1:T(8,128)(2,1)}, u32[]{:S(2)}, u32[]{:S(2)}) %all-to-all-start.2) | async-done | bytes 1048608 | tf_op jit(solution)/shard_map/all_to_all | solution.py:100
  74.3 3.5 %all-to-all-start.1 = ((bf16[128,4,1280]{2,0,1:T(8,128)(2,1)}), bf16[128,4,1280]{2,0,1:T(8,128)(2,1)S(1)}, u32[]{:S(2)}, u32[]{:S(2)}) async-start(bf16[128,4,1280]{2,0,1:T(8,128)(2,1)} %pad_maximum_fusion), calls=%async_computation.1 | async-start | bytes 2621440 | tf_op jit(solution)/shard_map/all_to_all | solution.py:81
  77.9 26.7 %all_gather.3 = s32[1,512]{1,0:T(1,128)S(1)} all-gather(s32[1,128]{1,0:T(1,128)S(1)} %copy-done.3), channel_id=1, replica_groups=mesh['grp'=2,'dp'=4,'sp'=4] {'sp'}, dimensions={1}, use_global_device_ids=true | all-gather | bytes 2560 | tf_op jit(solution)/shard_map/all_gather | solution.py:89
  104.8 2.6 %copy.83 = bf16[64,8,8,128]{3,2,1,0:T(8,128)(2,1)} copy(bf16[64,8,8,128]{3,1,2,0:T(8,128)(2,1)} %bitcast.57) | data formatting | bytes 2097152
  107.4 1.4 all-to-all-done.1
  109.9 1.5 copy.64
  111.4 1.5 fusion.4
  112.9 1.7 fusion.6
  114.7 3.0 %fusion = (f32[8,512]{1,0:T(8,128)S(1)}, f32[512,512,8]{1,0,2:T(8,128)S(1)}) fusion(f32[8,512]{1,0:T(8,128)S(1)} %fusion.6, f32[8,512]{1,0:T(8,128)S(1)} %get-tuple-element.52, f32[512,512,8]{1,0,2:T(8,128)S(1)} %get-tuple-element.53, pred[512,512]{0,1:T(8,128)(4,1)S(1)} %get-tuple-element.51, bf16[512,8,128]{2,1,0:T(8,128)(2,1)S(1)} %bitcast.141, ...), kind=kOutput, calls=%fused_computation.5 | convolution fusion | flops 549449728 | bytes 18268160 | tf_op jit(solution)/shard_map/bhd,kd->hbk/dot_general | solution.py:134
  117.7 4.6 %multiply_convert_fusion = (bf16[512,512,8]{1,0,2:T(8,128)(2,1)}, bf16[512,512,8]{1,0,2:T(8,128)(2,1)S(1)}) fusion(f32[512,512,8]{1,0,2:T(8,128)S(1)} %get-tuple-element.55, f32[512,8]{0,1:T(8,128)S(1)} %bitcast.150, f32[512,8]{0,1:T(8,128)S(1)} %bitcast.148, f32[512,8]{0,1:T(8,128)S(1)} %bitcast.147, f32[512,512,8]{1,0,2:T(8,128)S(1)} %get-tuple-element.53, ...), kind=kLoop, calls=%fused_computation.10 | loop fusion | flops 18874368 | bytes 25477120 | tf_op jit(solution)/shard_map/convert_element_type | solution.py:138
  122.3 3.6 %fusion.22 = bf16[4,128,128]{1,2,0:T(8,128)(2,1)S(1)} fusion(bf16[4,128,512,8]{2,1,0,3:T(8,128)(2,1)} %bitcast.143, bf16[512,8,128,1]{0,2,3,1:T(8,128)(2,1)S(1)} %bitcast.137), kind=kOutput, calls=%fused_computation.29 | convolution fusion | flops 536936448 | bytes 5373952 | tf_op jit(solution)/shard_map/hbk,bhd->kd/dot_general | solution.py:145
  125.9 1.5 fusion.23
  128.2 7.7 %all-to-all-start.4 = ((bf16[4,128,256]{1,2,0:T(8,128)(2,1)}), bf16[4,128,256]{1,2,0:T(8,128)(2,1)S(1)}, u32[]{:S(2)}, u32[]{:S(2)}) async-start(bf16[4,128,256]{1,2,0:T(8,128)(2,1)} %pad_maximum_fusion.1), calls=%async_computation.4 | async-start | bytes 524288 | tf_op jit(solution)/shard_map/all_to_all | solution.py:162
  135.8 7.8 %fusion.15 = bf16[512,8,128]{0,2,1:T(8,128)(2,1)S(1)} fusion(f32[512,512,8]{1,0,2:T(8,128)} %copy-done.1, f32[8,512]{1,0:T(8,128)S(1)} %get-tuple-element.54, f32[512,512,8]{1,0,2:T(8,128)} %copy-done, f32[8,512]{1,0:T(8,128)S(1)} %fusion.6, f32[8,512]{1,0:T(8,128)S(1)} %get-tuple-element.52, pred[512,512]{0,1:T(8,128)(4,1)S(1)} %get-tuple-element.51, ...), kind=kOutput, calls=%fused_computation.22 | convolution fusion | flops 554172416 | bytes 18268160 | tf_op jit(solution)/shard_map/hbk,kd->bhd/dot_general | solution.py:140
  145.1 5.1 %all-to-all-start.3 = ((bf16[4,128,1024]{1,2,0:T(8,128)(2,1)}), bf16[4,128,1024]{1,2,0:T(8,128)(2,1)S(1)}, u32[]{:S(2)}, u32[]{:S(2)}) async-start(bf16[4,128,1024]{1,2,0:T(8,128)(2,1)} %copy.70), calls=%async_computation.3 | async-start | bytes 2097152 | tf_op jit(solution)/shard_map/all_to_all | solution.py:158
  151.2 22.2 %all-to-all-done.3 = bf16[4,128,1024]{1,2,0:T(8,128)(2,1)S(1)} async-done(((bf16[4,128,1024]{1,2,0:T(8,128)(2,1)}), bf16[4,128,1024]{1,2,0:T(8,128)(2,1)S(1)}, u32[]{:S(2)}, u32[]{:S(2)}) %all-to-all-start.3) | async-done | bytes 1048608 | tf_op jit(solution)/shard_map/all_to_all | solution.py:158
  (50 shorter events, 12.7 us)
Async XLA Ops:
  0.6 14.8 %copy-start.5 = (s32[16]{0:T(128)S(1)}, s32[16]{0:T(128)}, u32[]{:S(2)}) copy-start(s32[16]{0:T(128)} %param.20) | copy-start | bytes 196
  0.6 14.8 %copy-start.4 = (s32[16]{0:T(128)S(1)}, s32[16]{0:T(128)}, u32[]{:S(2)}) copy-start(s32[16]{0:T(128)} %param.21) | copy-start | bytes 196
  0.7 15.1 %copy-start.3 = (s32[1,128]{1,0:T(1,128)S(1)}, s32[1,128]{1,0:T(1,128)}, u32[]{:S(2)}) copy-start(s32[1,128]{1,0:T(1,128)} %param.18) | copy-start | bytes 1540
  7.5 35.6 %all-to-all-start = ((bf16[4,64,5120]{2,1,0:T(8,128)(2,1)}), bf16[4,64,5120]{2,1,0:T(8,128)(2,1)S(1)}, u32[]{:S(2)}, u32[]{:S(2)}) async-start(bf16[4,64,5120]{2,1,0:T(8,128)(2,1)} %bitcast.131), calls=%async_computation | async-start | bytes 5242880 | tf_op jit(solution)/shard_map/all_to_all | solution.py:64
  43.1 31.2 %all-to-all-start.2 = ((bf16[128,4,1024]{2,0,1:T(8,128)(2,1)}), bf16[128,4,1024]{2,0,1:T(8,128)(2,1)}, u32[]{:S(2)}, u32[]{:S(2)}) async-start(bf16[128,4,1024]{2,0,1:T(8,128)(2,1)} %fusion.11), calls=%async_computation.2 | async-start | bytes 2097152 | tf_op jit(solution)/shard_map/all_to_all | solution.py:100
  74.3 34.4 %all-to-all-start.1 = ((bf16[128,4,1280]{2,0,1:T(8,128)(2,1)}), bf16[128,4,1280]{2,0,1:T(8,128)(2,1)S(1)}, u32[]{:S(2)}, u32[]{:S(2)}) async-start(bf16[128,4,1280]{2,0,1:T(8,128)(2,1)} %pad_maximum_fusion), calls=%async_computation.1 | async-start | bytes 2621440 | tf_op jit(solution)/shard_map/all_to_all | solution.py:81
  111.4 3.3 %copy-start.2 = (bf16[64,8,8,128]{3,2,1,0:T(8,128)(2,1)S(1)}, bf16[64,8,8,128]{3,2,1,0:T(8,128)(2,1)}, u32[]{:S(2)}) copy-start(bf16[64,8,8,128]{3,2,1,0:T(8,128)(2,1)} %copy.83) | copy-start | bytes 3145732
  112.9 4.8 %copy-start = (f32[512,512,8]{1,0,2:T(8,128)}, f32[512,512,8]{1,0,2:T(8,128)S(1)}, u32[]{:S(2)}) copy-start(f32[512,512,8]{1,0,2:T(8,128)S(1)} %get-tuple-element.53) | copy-start | bytes 25165828
  117.7 4.6 %copy-start.1 = (f32[512,512,8]{1,0,2:T(8,128)}, f32[512,512,8]{1,0,2:T(8,128)S(1)}, u32[]{:S(2)}) copy-start(f32[512,512,8]{1,0,2:T(8,128)S(1)} %get-tuple-element.55) | copy-start | bytes 25165828
  128.2 16.9 %all-to-all-start.4 = ((bf16[4,128,256]{1,2,0:T(8,128)(2,1)}), bf16[4,128,256]{1,2,0:T(8,128)(2,1)S(1)}, u32[]{:S(2)}, u32[]{:S(2)}) async-start(bf16[4,128,256]{1,2,0:T(8,128)(2,1)} %pad_maximum_fusion.1), calls=%async_computation.4 | async-start | bytes 524288 | tf_op jit(solution)/shard_map/all_to_all | solution.py:162
  145.1 28.4 %all-to-all-start.3 = ((bf16[4,128,1024]{1,2,0:T(8,128)(2,1)}), bf16[4,128,1024]{1,2,0:T(8,128)(2,1)S(1)}, u32[]{:S(2)}, u32[]{:S(2)}) async-start(bf16[4,128,1024]{1,2,0:T(8,128)(2,1)} %copy.70), calls=%async_computation.3 | async-start | bytes 2097152 | tf_op jit(solution)/shard_map/all_to_all | solution.py:158
where the time goes:
time: 176 us; the launch traced here: 175 us
  waiting for transfers between devices  64.2 us (36%)
  blocking collectives  26.7 us (15%)
  starting transfers between devices  26.2 us (15%)
  local copies, waits for them, and re-layouts  24.3 us (14%)
  matrix products  17.5 us (10%)
  other arithmetic  14.9 us (8%)
    all_gather x1, blocking collectives, body(): full_seg = lax.all_gather(segment_labels, 'sp', axis=1, tiled=True)[0]  26.7 us
    all_to_all x1, waiting for transfers between devices, body(): lax.all_to_all(outgoing.reshape(dp_size, capacity, row_width), 'dp', spli...  23.5 us
    all_to_all x1, waiting for transfers between devices, body(): lax.all_to_all(query_back, 'sp', split_axis=0, concat_axis=2, tiled=True)  22.2 us
    all_to_all x1, waiting for transfers between devices, body(): lax.all_to_all(weighted_result.reshape(token_rows, sequence_split_size, p...  17.1 us
    dot_general x1, matrix products, body(): jnp.einsum('hbk,kd->bhd', score_grads, key_part, preferred_element_type=j...  7.8 us
    all_to_all x1, starting transfers between devices, body(): lax.all_to_all(partial_value.astype(jnp.bfloat16), 'sp', split_axis=0, co...  7.66 us
    all_to_all x1, starting transfers between devices, body(): lax.all_to_all(weighted_result.reshape(token_rows, sequence_split_size, p...  5.68 us
    all_to_all x1, starting transfers between devices, body(): lax.all_to_all(query_back, 'sp', split_axis=0, concat_axis=2, tiled=True)  5.09 us
  transfers between devices with their start and end apart: 5, of which 4 were waited for; matrix products, arithmetic and copies ran while one was open for 17% of the time, Pallas kernels for 0%

commit v1 on v0

--- a/solution.py
+++ b/solution.py
@@ -155,7 +155,10 @@
     query_back = jnp.concatenate(query_parts, axis=0).reshape(
         sequence_split_size, token_rows, per_dev * HEAD_SIZE
     )
-    query_gradient = lax.all_to_all(query_back, "sp", split_axis=0, concat_axis=2, tiled=True)
+    query_gradient = jnp.concatenate(
+        lax.all_to_all(jnp.stack(jnp.split(query_back, lax.axis_size("sp"), axis=0)), "sp", 0, 0),
+        axis=2,
+    )
     partial_value = jnp.concatenate([key_total, value_total], axis=1).reshape(
         sequence_split_size, token_rows, 2 * HEAD_SIZE
     )

time: 176 us -> 175 us (level)
  waiting for transfers between devices: 64.2 us -> 68.3 us
  local copies, waits for them, and re-layouts: 24.3 us -> 21.1 us
  matrix products: 17.5 us -> 15.1 us
  other arithmetic: 14.9 us -> 16.8 us
    all_to_all x1, waiting for transfers between devices: 0.01 us -> 5.39 us  [body(): lax.all_to_all(partial_value.astype(jnp.bfloat16), 'sp', split_axis=0, co...]
    dot_general x1, matrix products: 7.8 us -> 4.3 us  [body(): jnp.einsum('hbk,kd->bhd', score_grads, key_part, preferred_element_type=j...]
    slice x2, local copies, waits for them, and re-layouts: 2.6 us -> 0.67 us  [body(): local_rows[:, :per_dev * HEAD_SIZE].reshape(seq_len, per_dev, HEAD_SIZE)]
    unnamed x14 -> x15, local copies, waits for them, and re-layouts: 3.9 us -> 2.5 us
  transfers between devices with their start and end apart: 5 -> 5, of which waited for: 4 -> 5; matrix products, arithmetic and copies ran while one was open for 17% -> 13% of each run, Pallas kernels for 0% -> 0%
where the time goes in v1:
time: 175 us; the launch traced here: 174 us
  waiting for transfers between devices  68.3 us (39%)
  blocking collectives  26.7 us (15%)
  starting transfers between devices  25.3 us (14%)
  local copies, waits for them, and re-layouts  21.1 us (12%)
  other arithmetic  16.8 us (10%)
  matrix products  15.1 us (9%)
    all_gather x1, blocking collectives, body(): full_seg = lax.all_gather(segment_labels, 'sp', axis=1, tiled=True)[0]  26.7 us
    all_to_all x1, waiting for transfers between devices, body(): lax.all_to_all(outgoing.reshape(dp_size, capacity, row_width), 'dp', spli...  23.5 us
    all_to_all x1, waiting for transfers between devices, body(): lax.all_to_all(jnp.stack(jnp.split(query_back, lax.axis_size('sp'), axis=...  21.6 us
    all_to_all x1, waiting for transfers between devices, body(): lax.all_to_all(weighted_result.reshape(token_rows, sequence_split_size, p...  17.1 us
    all_to_all x1, starting transfers between devices, body(): lax.all_to_all(partial_value.astype(jnp.bfloat16), 'sp', split_axis=0, co...  8.34 us
    all_to_all x1, starting transfers between devices, body(): lax.all_to_all(weighted_result.reshape(token_rows, sequence_split_size, p...  5.68 us
    all_to_all x1, waiting for transfers between devices, body(): lax.all_to_all(partial_value.astype(jnp.bfloat16), 'sp', split_axis=0, co...  5.39 us
    scatter x1, local copies, waits for them, and re-layouts, body(): outgoing = jnp.zeros((dp_size * capacity, row_width), rollout_rows.dtype)...  5.01 us
  transfers between devices with their start and end apart: 5, of which 5 were waited for; matrix products, arithmetic and copies ran while one was open for 13% of the time, Pallas kernels for 0%

profile of v1, /device:TPU:0, one launch (start us, length us, event | category | flops | bytes accessed | tf_op | source)
XLA Modules:
  0.0 174.3 jit_solution(14704799677196582048)
XLA Ops:
  2.5 5.0 %scatter_custom_fusion = bf16[256,5120]{1,0:T(8,128)(2,1)} fusion(s32[128]{0:T(128)S(1)} %fusion.32, bf16[128,5120]{1,0:T(8,128)(2,1)} %param.16, bf16[]{:T(256)} %constant.129.clone.1), kind=kCustom, calls=%fused_computation.24 | custom fusion | bytes 2621952 | tf_op jit(solution)/shard_map/scatter | solution.py:62
  7.5 4.2 %all-to-all-start = ((bf16[4,64,5120]{2,1,0:T(8,128)(2,1)}), bf16[4,64,5120]{2,1,0:T(8,128)(2,1)S(1)}, u32[]{:S(2)}, u32[]{:S(2)}) async-start(bf16[4,64,5120]{2,1,0:T(8,128)(2,1)} %bitcast.131), calls=%async_computation | async-start | bytes 5242880 | tf_op jit(solution)/shard_map/all_to_all | solution.py:64
  11.8 3.7 %reshape.292 = f32[128,4,1024]{2,1,0:T(4,128)} reshape(bf16[1,128,4096]{2,1,0:T(8,128)(2,1)} %param.19) | data formatting | bytes 3145728 | tf_op jit(solution)/shard_map/convert_element_type | solution.py:99
  15.9 3.7 %fusion.11 = bf16[128,4,1024]{2,0,1:T(8,128)(2,1)} fusion(f32[128,4,1024]{2,1,0:T(4,128)} %reshape.292, f32[128]{0:T(128)S(1)} %select_reduce_fusion.2), kind=kLoop, calls=%fused_computation.20 | loop fusion | flops 1048576 | bytes 3146240 | tf_op jit(solution)/shard_map/convert_element_type | solution.py:99
  19.6 23.5 %all-to-all-done = bf16[4,64,5120]{2,1,0:T(8,128)(2,1)S(1)} async-done(((bf16[4,64,5120]{2,1,0:T(8,128)(2,1)}), bf16[4,64,5120]{2,1,0:T(8,128)(2,1)S(1)}, u32[]{:S(2)}, u32[]{:S(2)}) %all-to-all-start) | async-done | bytes 2621472 | tf_op jit(solution)/shard_map/all_to_all | solution.py:64
  43.1 5.7 %all-to-all-start.2 = ((bf16[128,4,1024]{2,0,1:T(8,128)(2,1)}), bf16[128,4,1024]{2,0,1:T(8,128)(2,1)}, u32[]{:S(2)}, u32[]{:S(2)}) async-start(bf16[128,4,1024]{2,0,1:T(8,128)(2,1)} %fusion.11), calls=%async_computation.2 | async-start | bytes 2097152 | tf_op jit(solution)/shard_map/all_to_all | solution.py:100
  50.1 2.4 %gather_fusion = bf16[128,5120]{1,0:T(8,128)(2,1)} fusion(bf16[256,5120]{1,0:T(8,128)(2,1)S(1)} %bitcast.129, s32[1024]{0:T(1024)S(1)} %pad_clamp_fusion.1), kind=kCustom, calls=%fused_computation | custom fusion | bytes 2621952 | tf_op jit(solution)/shard_map/gather | solution.py:78
  53.5 1.3 slice.56
  57.2 17.1 %all-to-all-done.2 = bf16[128,4,1024]{2,0,1:T(8,128)(2,1)} async-done(((bf16[128,4,1024]{2,0,1:T(8,128)(2,1)}), bf16[128,4,1024]{2,0,1:T(8,128)(2,1)}, u32[]{:S(2)}, u32[]{:S(2)}) %all-to-all-start.2) | async-done | bytes 1048608 | tf_op jit(solution)/shard_map/all_to_all | solution.py:100
  74.3 3.5 %all-to-all-start.1 = ((bf16[128,4,1280]{2,0,1:T(8,128)(2,1)}), bf16[128,4,1280]{2,0,1:T(8,128)(2,1)S(1)}, u32[]{:S(2)}, u32[]{:S(2)}) async-start(bf16[128,4,1280]{2,0,1:T(8,128)(2,1)} %pad_maximum_fusion), calls=%async_computation.1 | async-start | bytes 2621440 | tf_op jit(solution)/shard_map/all_to_all | solution.py:81
  77.9 26.7 %all_gather.3 = s32[1,512]{1,0:T(1,128)S(1)} all-gather(s32[1,128]{1,0:T(1,128)S(1)} %copy-done.4), channel_id=1, replica_groups=mesh['grp'=2,'dp'=4,'sp'=4] {'sp'}, dimensions={1}, use_global_device_ids=true | all-gather | bytes 2560 | tf_op jit(solution)/shard_map/all_gather | solution.py:89
  105.6 2.5 %copy.69 = bf16[64,8,8,128]{3,2,1,0:T(8,128)(2,1)} copy(bf16[64,8,8,128]{3,1,2,0:T(8,128)(2,1)} %bitcast.59) | data formatting | bytes 2097152
  109.5 2.6 %fusion.4 = (f32[8,512]{1,0:T(8,128)S(1)}, f32[512,512,8]{1,0,2:T(8,128)S(1)}) fusion(pred[512,512]{0,1:T(8,128)(4,1)} %get-tuple-element.51, bf16[512,8,128]{0,2,1:T(8,128)(2,1)S(1)} %bitcast.136, bf16[512,1280]{1,0:T(8,128)(2,1)S(1)} %bitcast.133), kind=kOutput, calls=%fused_computation.13 | convolution fusion | flops 543158272 | bytes 9846784 | tf_op jit(solution)/shard_map/bhd,kd->hbk/dot_general | solution.py:124
  112.1 1.8 %fusion.6 = f32[8,512]{1,0:T(8,128)S(1)} fusion(f32[512,512,8]{1,0,2:T(8,128)S(1)} %get-tuple-element.53, f32[8,512]{1,0:T(8,128)S(1)} %get-tuple-element.52, pred[512,512]{0,1:T(8,128)(4,1)S(1)} %copy-done.1), kind=kLoop, calls=%fused_computation.15 | loop fusion | flops 8384512 | bytes 8683520 | tf_op jit(solution)/shard_map/reduce_sum | solution.py:133
  113.8 3.0 %fusion = (f32[8,512]{1,0:T(8,128)S(1)}, f32[512,512,8]{1,0,2:T(8,128)S(1)}) fusion(f32[8,512]{1,0:T(8,128)S(1)} %fusion.6, f32[8,512]{1,0:T(8,128)S(1)} %get-tuple-element.52, f32[512,512,8]{1,0,2:T(8,128)S(1)} %get-tuple-element.53, pred[512,512]{0,1:T(8,128)(4,1)S(1)} %copy-done.1, bf16[512,8,128]{2,1,0:T(8,128)(2,1)S(1)} %bitcast.141, ...), kind=kOutput, calls=%fused_computation.5 | convolution fusion | flops 549449728 | bytes 18268160 | tf_op jit(solution)/shard_map/bhd,kd->hbk/dot_general | solution.py:134
  116.8 4.3 %fusion.15 = bf16[512,8,128]{0,2,1:T(8,128)(2,1)} fusion(f32[512,512,8]{1,0,2:T(8,128)S(1)} %get-tuple-element.55, f32[8,512]{1,0:T(8,128)S(1)} %get-tuple-element.54, f32[512,512,8]{1,0,2:T(8,128)S(1)} %get-tuple-element.53, f32[8,512]{1,0:T(8,128)S(1)} %fusion.6, f32[8,512]{1,0:T(8,128)S(1)} %get-tuple-element.52, pred[512,512]{0,1:T(8,128)(4,1)S(1)} %copy-done.1, ...), kind=kOutput, calls=%fused_computation.22 | convolution fusion | flops 554172416 | bytes 18268160 | tf_op jit(solution)/shard_map/hbk,kd->bhd/dot_general | solution.py:140
  121.2 4.6 %multiply_convert_fusion = (bf16[512,512,8]{1,0,2:T(8,128)(2,1)}, bf16[512,512,8]{1,0,2:T(8,128)(2,1)S(1)}) fusion(f32[512,512,8]{1,0,2:T(8,128)S(1)} %get-tuple-element.55, f32[512,8]{0,1:T(8,128)S(1)} %bitcast.154, f32[512,8]{0,1:T(8,128)S(1)} %bitcast.152, f32[512,8]{0,1:T(8,128)S(1)} %bitcast.151, f32[512,512,8]{1,0,2:T(8,128)S(1)} %get-tuple-element.53, ...), kind=kLoop, calls=%fused_computation.10 | loop fusion | flops 18874368 | bytes 25477120 | tf_op jit(solution)/shard_map/convert_element_type | solution.py:138
  125.7 3.7 %fusion.22 = bf16[4,128,128]{1,2,0:T(8,128)(2,1)S(1)} fusion(bf16[4,128,512,8]{2,1,0,3:T(8,128)(2,1)} %bitcast.143, bf16[512,8,128,1]{0,2,3,1:T(8,128)(2,1)S(1)} %bitcast.137), kind=kOutput, calls=%fused_computation.29 | convolution fusion | flops 536936448 | bytes 5373952 | tf_op jit(solution)/shard_map/hbk,bhd->kd/dot_general | solution.py:145
  129.4 1.5 fusion.23
  131.7 8.3 %all-to-all-start.4 = ((bf16[4,128,256]{1,2,0:T(8,128)(2,1)}), bf16[4,128,256]{1,2,0:T(8,128)(2,1)S(1)}, u32[]{:S(2)}, u32[]{:S(2)}) async-start(bf16[4,128,256]{1,2,0:T(8,128)(2,1)} %pad_maximum_fusion.2), calls=%async_computation.4 | async-start | bytes 524288 | tf_op jit(solution)/shard_map/all_to_all | solution.py:165
  141.4 5.4 %all-to-all-done.4 = bf16[4,128,256]{1,2,0:T(8,128)(2,1)S(1)} async-done(((bf16[4,128,256]{1,2,0:T(8,128)(2,1)}), bf16[4,128,256]{1,2,0:T(8,128)(2,1)S(1)}, u32[]{:S(2)}, u32[]{:S(2)}) %all-to-all-start.4) | async-done | bytes 262176 | tf_op jit(solution)/shard_map/all_to_all | solution.py:165
  146.8 3.5 %all-to-all-start.3 = ((bf16[4,1,128,1024]{2,3,1,0:T(8,128)(2,1)}), bf16[4,1,128,1024]{2,3,1,0:T(8,128)(2,1)S(1)}, u32[]{:S(2)}, u32[]{:S(2)}) async-start(bf16[4,1,128,1024]{2,3,1,0:T(8,128)(2,1)} %pad_maximum_fusion.1), calls=%async_computation.3 | async-start | bytes 2097152 | tf_op jit(solution)/shard_map/all_to_all | solution.py:159
  151.4 21.6 %all-to-all-done.3 = bf16[4,1,128,1024]{2,3,1,0:T(8,128)(2,1)S(1)} async-done(((bf16[4,1,128,1024]{2,3,1,0:T(8,128)(2,1)}), bf16[4,1,128,1024]{2,3,1,0:T(8,128)(2,1)S(1)}, u32[]{:S(2)}, u32[]{:S(2)}) %all-to-all-start.3) | async-done | bytes 1048608 | tf_op jit(solution)/shard_map/all_to_all | solution.py:159
  173.0 1.3 copy.65
  (52 shorter events, 12.5 us)
Async XLA Ops:
  0.6 14.8 %copy-start.6 = (s32[16]{0:T(128)S(1)}, s32[16]{0:T(128)}, u32[]{:S(2)}) copy-start(s32[16]{0:T(128)} %param.20) | copy-start | bytes 196
  0.6 14.8 %copy-start.5 = (s32[16]{0:T(128)S(1)}, s32[16]{0:T(128)}, u32[]{:S(2)}) copy-start(s32[16]{0:T(128)} %param.21) | copy-start | bytes 196
  0.7 15.1 %copy-start.4 = (s32[1,128]{1,0:T(1,128)S(1)}, s32[1,128]{1,0:T(1,128)}, u32[]{:S(2)}) copy-start(s32[1,128]{1,0:T(1,128)} %param.18) | copy-start | bytes 1540
  7.5 35.6 %all-to-all-start = ((bf16[4,64,5120]{2,1,0:T(8,128)(2,1)}), bf16[4,64,5120]{2,1,0:T(8,128)(2,1)S(1)}, u32[]{:S(2)}, u32[]{:S(2)}) async-start(bf16[4,64,5120]{2,1,0:T(8,128)(2,1)} %bitcast.131), calls=%async_computation | async-start | bytes 5242880 | tf_op jit(solution)/shard_map/all_to_all | solution.py:64
  43.1 31.2 %all-to-all-start.2 = ((bf16[128,4,1024]{2,0,1:T(8,128)(2,1)}), bf16[128,4,1024]{2,0,1:T(8,128)(2,1)}, u32[]{:S(2)}, u32[]{:S(2)}) async-start(bf16[128,4,1024]{2,0,1:T(8,128)(2,1)} %fusion.11), calls=%async_computation.2 | async-start | bytes 2097152 | tf_op jit(solution)/shard_map/all_to_all | solution.py:100
  74.3 34.4 %all-to-all-start.1 = ((bf16[128,4,1280]{2,0,1:T(8,128)(2,1)}), bf16[128,4,1280]{2,0,1:T(8,128)(2,1)S(1)}, u32[]{:S(2)}, u32[]{:S(2)}) async-start(bf16[128,4,1280]{2,0,1:T(8,128)(2,1)} %pad_maximum_fusion), calls=%async_computation.1 | async-start | bytes 2621440 | tf_op jit(solution)/shard_map/all_to_all | solution.py:81
  109.4 2.6 %copy-start.1 = (pred[512,512]{0,1:T(8,128)(4,1)S(1)}, pred[512,512]{0,1:T(8,128)(4,1)}, u32[]{:S(2)}) copy-start(pred[512,512]{0,1:T(8,128)(4,1)} %get-tuple-element.51) | copy-start | bytes 786436
  109.5 4.4 %copy-start = (bf16[64,8,8,128]{3,2,1,0:T(8,128)(2,1)S(1)}, bf16[64,8,8,128]{3,2,1,0:T(8,128)(2,1)}, u32[]{:S(2)}) copy-start(bf16[64,8,8,128]{3,2,1,0:T(8,128)(2,1)} %copy.69) | copy-start | bytes 3145732
  116.8 4.3 %copy-start.2 = (pred[512,512]{1,0:T(8,128)(4,1)S(1)}, pred[512,512]{1,0:T(8,128)(4,1)}, u32[]{:S(2)}) copy-start(pred[512,512]{1,0:T(8,128)(4,1)} %get-tuple-element.50) | copy-start | bytes 786436
  125.7 14.3 %copy-start.3 = (bf16[512,8,128]{0,2,1:T(8,128)(2,1)S(1)}, bf16[512,8,128]{0,2,1:T(8,128)(2,1)}, u32[]{:S(2)}) copy-start(bf16[512,8,128]{0,2,1:T(8,128)(2,1)} %fusion.15) | copy-start | bytes 3145732
  131.7 15.1 %all-to-all-start.4 = ((bf16[4,128,256]{1,2,0:T(8,128)(2,1)}), bf16[4,128,256]{1,2,0:T(8,128)(2,1)S(1)}, u32[]{:S(2)}, u32[]{:S(2)}) async-start(bf16[4,128,256]{1,2,0:T(8,128)(2,1)} %pad_maximum_fusion.2), calls=%async_computation.4 | async-start | bytes 524288 | tf_op jit(solution)/shard_map/all_to_all | solution.py:165
  146.8 26.2 %all-to-all-start.3 = ((bf16[4,1,128,1024]{2,3,1,0:T(8,128)(2,1)}), bf16[4,1,128,1024]{2,3,1,0:T(8,128)(2,1)S(1)}, u32[]{:S(2)}, u32[]{:S(2)}) async-start(bf16[4,1,128,1024]{2,3,1,0:T(8,128)(2,1)} %pad_maximum_fusion.1), calls=%async_computation.3 | async-start | bytes 2097152 | tf_op jit(solution)/shard_map/all_to_all | solution.py:159
